TPU v7x, 512 devices: a whole 4x4x16 slice. The times are simulated.
512 devices in a mesh: smp: 16 (over z), par: 32 (over x, y, core).
Axes of the slice: x: 4, y: 4, z: 16, core: 2. Of those that a mesh axis runs over, the one named last changes fastest.
Arguments:
- jacobian: bfloat16 [4096, 16384], P('smp', 'par'), may hold values from -52 to 52
Outputs:
- panel_factor: float32 [4096, 512], P('smp')
- schur_part: float32 [4096, 4096], P('smp', 'par')
All inputs are finite; a program needn't handle non-finite values.
Results may differ from a plain program's by a relative error of at most 0.0022.
Values may be sent and summed in bfloat16 or wider, within the bound.
No kernel may reach another device: no remote copies, remote signals or barrier semaphores. Data moves between devices by JAX's collectives and lax.ppermute only.
A program may use at most 64 MiB of HBM per device.

v0:
```python
import jax
import jax.numpy as jnp
from jax import lax
from jax.sharding import PartitionSpec as P

PANEL = 512
shift_scale = 0.01


def shards(jacobian):
    row_count, par_width = jacobian.shape
    par_count = lax.axis_size("par")
    smp_count = lax.axis_size("smp")
    sample_total = row_count * smp_count
    param_total = par_width * par_count
    col_width = sample_total // par_count
    panel_piece = PANEL // par_count
    row_index = lax.axis_index("smp")
    col_index = lax.axis_index("par")
    f32 = jnp.float32
    gathered = lax.all_gather(jacobian, "smp", axis=0, tiled=True)
    widened = gathered.astype(f32)
    col_mean = jnp.sum(widened, axis=0) / sample_total
    centered = (widened - col_mean).astype(jnp.bfloat16)
    mine = lax.dynamic_slice_in_dim(centered, row_index * row_count, row_count, 0)
    head = centered[:PANEL]
    contract = (((1,), (1,)), ((), ()))
    main = lax.dot_general(centered, mine, contract, preferred_element_type=f32)
    square = lax.dot_general(head, head, contract, preferred_element_type=f32)
    band = lax.dot_general(centered, head, contract, preferred_element_type=f32)
    sq = centered.astype(f32)
    sumsq = jnp.sum(sq * sq)
    width = row_count
    panel_parts = jnp.concatenate(
        [
            main[:PANEL].reshape(par_count, panel_piece, width),
            square.reshape(par_count, panel_piece * PANEL // width, width),
            jnp.broadcast_to(sumsq, (par_count, 8, width)),
        ],
        axis=1,
    )
    chunk = panel_parts.shape[1]
    reduced = (
        lax.psum_scatter(
            panel_parts.reshape(par_count * chunk, width), "par", scatter_dimension=0, tiled=True
        )
        / param_total
    )
    shared = lax.all_gather(reduced, "par", axis=0, tiled=False)
    main_parts = jnp.concatenate(
        [
            main.reshape(par_count, col_width, width),
            band.reshape(par_count, col_width * PANEL // width, width),
        ],
        axis=1,
    )
    main_parts, shared = lax.optimization_barrier((main_parts, shared))
    main_chunk = main_parts.shape[1]
    reduced_main = (
        lax.psum_scatter(
            main_parts.reshape(par_count * main_chunk, width),
            "par",
            scatter_dimension=0,
            tiled=True,
        )
        / param_total
    )
    tile = reduced_main[:col_width].T
    band_mine = reduced_main[col_width:].reshape(col_width, PANEL)
    o2 = panel_piece
    o3 = o2 + panel_piece * PANEL // width
    panel_t = shared[:, :o2].reshape(PANEL, width)
    square_g = shared[:, o2:o3].reshape(PANEL, PANEL)
    trace_total = shared[0, o3, 0]
    shift_value = shift_scale * trace_total / sample_total
    eye = jnp.arange(PANEL, dtype=jnp.int32)
    global_rows = row_index * row_count + jnp.arange(row_count, dtype=jnp.int32)
    global_cols = col_index * col_width + jnp.arange(col_width, dtype=jnp.int32)
    square_s = square_g + jnp.where(eye[:, None] == eye[None, :], shift_value, 0.0)
    panel_s = panel_t.T + jnp.where(global_rows[:, None] == eye[None, :], shift_value, 0.0)
    band_s = band_mine + jnp.where(global_cols[:, None] == eye[None, :], shift_value, 0.0)
    tile_s = tile + jnp.where(global_rows[:, None] == global_cols[None, :], shift_value, 0.0)
    factor = jnp.linalg.cholesky(square_s)
    panel_out = jax.scipy.linalg.solve_triangular(factor, panel_s.T, lower=True).T
    band_factor = jax.scipy.linalg.solve_triangular(factor, band_s.T, lower=True)
    schur_tile = tile_s - jnp.dot(panel_out, band_factor, precision=lax.Precision.HIGHEST)
    return (panel_out, schur_tile)


def solution(mesh):
    placed = (P("smp", "par"),)
    return jax.shard_map(
        shards,
        mesh=mesh,
        in_specs=placed,
        out_specs=(P("smp", None), P("smp", "par")),
        check_vma=False,
    )
```

profile of v0, /device:TPU:1, one launch (start us, length us, event | category | flops | bytes accessed | tf_op | source)
XLA Modules:
  0.0 437.3 jit_solution(6986741140144333234)
XLA Ops:
  7.2 0.7 all-gather.4.cloned.1.call-update
  7.9 77.4 %all-gather.4.cloned.1.call-done = bf16[4096,512]{1,0:T(8,128)(2,1)} async-done(((bf16[256,512]{1,0:T(8,128)(2,1)}), bf16[4096,512]{1,0:T(8,128)(2,1)}) %all-gather.4.cloned.1.call-update) | async-done | bytes 4194320 | tf_op jit(solution)/shard_map/all_gather | solution.py:21
  85.3 3.0 convert_reduce_fusion
  88.3 0.5 copy-done.2
  88.8 2.8 multiply_reduce_fusion
  91.6 2.0 copy-done
  93.5 0.5 fusion.2
  94.2 3.5 fusion.23
  97.7 1.9 copy-done.1
  99.7 0.6 broadcast_in_dim.46
  100.4 1.5 maximum_maximum_fusion
  102.0 105.5 %reduce-scatter.3.cloned.1.call-done = f32[56,256]{1,0:T(8,128)} async-done(((f32[1792,256]{1,0:T(8,128)}), f32[56,256]{1,0:T(8,128)}) %reduce-scatter.3.cloned.1.call-update) | async-done | bytes 57360 | tf_op jit(solution)/shard_map/reduce_scatter | solution.py:44
  207.5 1.4 broadcast_multiply_fusion.1
  209.0 8.0 %fusion.4 = f32[4096,512]{1,0:T(8,128)} fusion(bf16[4096,512]{1,0:T(8,128)(2,1)} %copy-done), kind=kOutput, calls=%fused_computation.31 | convolution fusion | flops 2147483648 | bytes 13107200 | tf_op jit(solution)/shard_map/dot_general | solution.py:30
  217.0 9.3 %reshape.100 = f32[32,256,256]{2,1,0:T(8,128)} reshape(f32[4096,512]{1,0:T(8,128)} %fusion.4) | data formatting | bytes 16777216 | tf_op jit(solution)/shard_map/reshape | solution.py:53
  226.3 10.5 %pad_maximum_fusion = f32[32,384,256]{2,1,0:T(8,128)} fusion(f32[32,256,256]{2,1,0:T(8,128)} %reshape.100, f32[32,128,256]{2,1,0:T(8,128)} %bitcast.75), kind=kLoop, calls=%fused_computation.2 | loop fusion | flops 3145728 | bytes 25165824 | tf_op jit(solution)/shard_map/concatenate | solution.py:50
  236.8 34.7 %all-gather.6.cloned.1.call-done = f32[1792,256]{1,0:T(8,128)} async-done(((f32[56,256]{1,0:T(8,128)}), f32[1792,256]{1,0:T(8,128)}) %all-gather.6.cloned.1.call-update) | async-done | bytes 1835024 | tf_op jit(solution)/shard_map/all_gather | solution.py:49
  271.5 13.1 %copy.29 = f32[12288,256]{0,1:T(8,128)} copy(f32[12288,256]{1,0:T(8,128)} %bitcast.74) | data formatting | bytes 25165824 | tf_op jit(solution)/shard_map/reshape | solution.py:61
  284.7 1.4 copy-done.4
  286.1 0.5 slice.171
  286.6 0.9 slice.172
  289.6 11.7 %cholesky.103 = f32[128,128]{1,0:T(8,128)S(1)} custom-call(f32[128,128]{1,0:T(8,128)S(1)} %cholesky.263), custom_call_target="Cholesky" | custom-call | tf_op jit(solution)/shard_map/jit(cholesky)/cholesky | solution.py:83
  301.5 9.8 %custom-call.34 = f32[1,128,128]{1,2,0:T(8,128)S(1)} custom-call(f32[1,128,128]{2,1,0:T(8,128)S(1)} %get-tuple-element.43), custom_call_target="InvertDiagBlocksLowerTriangular" | custom-call | tf_op jit(solution)/shard_map/jit(cholesky)/cholesky | solution.py:83
  312.1 11.7 %cholesky.215 = f32[128,128]{1,0:T(8,128)S(1)} custom-call(f32[128,128]{1,0:T(8,128)S(1)} %cholesky.267), custom_call_target="Cholesky" | custom-call | tf_op jit(solution)/shard_map/jit(cholesky)/cholesky | solution.py:83
  323.9 9.9 %custom-call.35 = f32[1,128,128]{1,2,0:T(8,128)S(1)} custom-call(f32[1,128,128]{2,1,0:T(8,128)S(1)} %get-tuple-element.41), custom_call_target="InvertDiagBlocksLowerTriangular" | custom-call | tf_op jit(solution)/shard_map/jit(cholesky)/cholesky | solution.py:83
  334.4 0.6 convolution_subtract_fusion.4
  335.0 11.7 %cholesky.236 = f32[128,128]{1,0:T(8,128)S(1)} custom-call(f32[128,128]{1,0:T(8,128)S(1)} %cholesky.272), custom_call_target="Cholesky" | custom-call | tf_op jit(solution)/shard_map/jit(cholesky)/cholesky | solution.py:83
  346.8 9.8 %custom-call.36 = f32[1,128,128]{1,2,0:T(8,128)S(1)} custom-call(f32[1,128,128]{2,1,0:T(8,128)S(1)} %get-tuple-element.39), custom_call_target="InvertDiagBlocksLowerTriangular" | custom-call | tf_op jit(solution)/shard_map/jit(cholesky)/cholesky | solution.py:83
  357.0 0.5 convolution_subtract_fusion.9
  357.5 11.9 %cholesky.253 = f32[128,128]{1,0:T(8,128)S(1)} custom-call(f32[128,128]{1,0:T(8,128)S(1)} %convolution_subtract_fusion.9), custom_call_target="Cholesky" | custom-call | tf_op jit(solution)/shard_map/jit(cholesky)/cholesky | solution.py:83
  369.5 0.6 compare_reduce_fusion.2
  371.3 0.6 compare_reduce_fusion.1
  372.7 0.6 compare_reduce_fusion
  374.1 8.1 %while.1 = (s32[]{:T(128)}, f32[512,512]{0,1:T(8,128)S(1)}, s32[4,2]{0,1:T(2,128)S(1)}, f32[4,128,128]{2,1,0:T(8,128)S(1)}, s32[]{:T(128)}) while((s32[]{:T(128)}, f32[512,512]{0,1:T(8,128)S(1)}, s32[4,2]{0,1:T(2,128)S(1)}, f32[4,128,128]{2,1,0:T(8,128)S(1)}, s32[]{:T(128)}) %tuple.34), condition=%wide.while_cond, body=%wide.while_body.sunk | while | flops 2 | bytes 393329 | solution.py:84
  374.2 0.5 fusion.80
  374.7 1.3 dynamic-slice.7
  376.2 0.5 fusion.80
  376.8 1.3 dynamic-slice.7
  378.3 0.5 fusion.80
  378.8 1.3 dynamic-slice.7
  380.3 0.5 fusion.80
  380.8 1.3 dynamic-slice.7
  382.2 39.3 %custom-call.37 = f32[4,128,128]{1,2,0:T(8,128)S(1)} custom-call(f32[4,128,128]{2,1,0:T(8,128)S(1)} %get-tuple-element.13), custom_call_target="InvertDiagBlocksLowerTriangular" | custom-call | tf_op jit(solution)/shard_map/jit(_solve_triangular)/triangular_solve | solution.py:84
  423.3 0.5 convolution_subtract_fusion.2
  424.2 1.0 copy.26
  425.2 1.0 broadcast_multiply_fusion
  428.1 0.5 convolution_subtract_fusion.8
  428.9 1.7 convolution_subtract_fusion.1
  (81 shorter events, 9.0 us)
Async XLA Ops:
  7.2 78.2 %all-gather.4.cloned.1.call-start = ((), (), s32[]{:S(2)}) async-start(), calls=%async_computation.2 | async-start | bytes 4456448 | tf_op jit(solution)/shard_map/all_gather | solution.py:21
  7.9 199.6 %reduce-scatter.3.cloned.1.call-start = ((), (), s32[]{:S(2)}) async-start(), calls=%async_computation.3 | async-start | bytes 1892352 | tf_op jit(solution)/shard_map/reduce_scatter | solution.py:44
  85.3 3.4 copy-start.2
  91.6 2.0 copy-start
  97.7 1.9 copy-start.1
  101.9 169.6 %all-gather.6.cloned.1.call-start = ((), (), s32[]{:S(2)}) async-start(), calls=%async_computation.5 | async-start | bytes 1892352 | tf_op jit(solution)/shard_map/all_gather | solution.py:49
  208.9 216.2 %reduce-scatter.5.cloned.1.call-start = ((), (), s32[]{:S(2)}) async-start(), calls=%async_computation.4 | async-start | bytes 12976128 | tf_op jit(solution)/shard_map/reduce_scatter | solution.py:60
  284.6 1.5 copy-start.4
  323.9 97.7 %copy-start.3 = (f32[32,16,256]{2,1,0:T(8,128)S(1)}, f32[32,16,256]{2,1,0:T(8,128)}, u32[]{:S(2)}) copy-start(f32[32,16,256]{2,1,0:T(8,128)} %slice.172) | copy-start | bytes 1572868
Sparse Core Ops, SparseCore 0:
  10.1 75.2 all-gather.3
  102.1 105.3 reduce-scatter.2
  211.2 60.3 all-gather.5
  284.8 125.7 reduce-scatter.4
where the time goes:
time: 444 us; the launch traced here: 437 us
  waiting for transfers between devices  218 us (49%)
  other arithmetic  139 us (31%)
  local copies, waits for them, and re-layouts  41.5 us (9%)
  matrix products  20.7 us (5%)
  between operations  17.7 us (4%)
    reduce_scatter x1, waiting for transfers between devices, shards(): lax.psum_scatter(panel_parts.reshape(par_count * chunk, width), 'par', sc...  105 us
    another operation x14, other arithmetic, shards(): factor = jnp.linalg.cholesky(square_s)  78.7 us
    all_gather x1, waiting for transfers between devices, shards(): gathered = lax.all_gather(jacobian, 'smp', axis=0, tiled=True)  77.4 us
    another operation x3, other arithmetic, shards(): jax.scipy.linalg.solve_triangular(factor, panel_s.T, lower=True)  39.5 us
    all_gather x1, waiting for transfers between devices, shards(): shared = lax.all_gather(reduced, 'par', axis=0, tiled=False)  34.7 us
    reshape x1, local copies, waits for them, and re-layouts, shards(): main_parts.reshape(par_count * main_chunk, width)  13.1 us
    concatenate x1, other arithmetic, shards(): jnp.concatenate([main.reshape(par_count, col_width, width), band.reshape(...  10.5 us
    reshape x1, local copies, waits for them, and re-layouts, shards(): band.reshape(par_count, col_width * PANEL // width, width)  9.33 us
  transfers between devices with their start and end apart: 4, of which 3 were waited for; matrix products, arithmetic and copies ran while one was open for 37% of the time, Pallas kernels for 0%

commit v1 on v0

--- a/solution.py
+++ b/solution.py
@@ -18,7 +18,10 @@
     row_index = lax.axis_index("smp")
     col_index = lax.axis_index("par")
     f32 = jnp.float32
-    gathered = lax.all_gather(jacobian, "smp", axis=0, tiled=True)
+    n_dev = lax.axis_size("smp")
+    shards_2 = jnp.stack([jacobian for _ in range(n_dev)])
+    shards_2 = lax.all_to_all(shards_2, "smp", split_axis=0, concat_axis=0)
+    gathered = jnp.concatenate(shards_2, axis=0)
     widened = gathered.astype(f32)
     col_mean = jnp.sum(widened, axis=0) / sample_total
     centered = (widened - col_mean).astype(jnp.bfloat16)

time: 444 us -> 568 us (1.28)
  waiting for transfers between devices: 218 us -> 317 us
  starting transfers between devices: 0.16 us -> 15.9 us
    all_to_all x0 -> x1, waiting for transfers between devices: none -> 182 us  [shards(): shards_2 = lax.all_to_all(shards_2, 'smp', split_axis=0, concat_axis=0)]
    all_gather x1 -> x0, waiting for transfers between devices: 77.4 us -> none  [shards(): gathered = lax.all_gather(jacobian, 'smp', axis=0, tiled=True)]
    all_to_all x0 -> x1, starting transfers between devices: none -> 15.8 us  [shards(): shards_2 = lax.all_to_all(shards_2, 'smp', split_axis=0, concat_axis=0)]
  transfers between devices with their start and end apart: 4 -> 4, of which waited for: 3 -> 3; matrix products, arithmetic and copies ran while one was open for 37% -> 29% of each run, Pallas kernels for 0% -> 0%
where the time goes in v1:
time: 568 us; the launch traced here: 560 us
  waiting for transfers between devices  317 us (56%)
  other arithmetic  144 us (25%)
  local copies, waits for them, and re-layouts  44.4 us (8%)
  matrix products  20.7 us (4%)
  between operations  17.7 us (3%)
  starting transfers between devices  15.9 us (3%)
    all_to_all x1, waiting for transfers between devices, shards(): shards_2 = lax.all_to_all(shards_2, 'smp', split_axis=0, concat_axis=0)  182 us
    reduce_scatter x1, waiting for transfers between devices, shards(): lax.psum_scatter(panel_parts.reshape(par_count * chunk, width), 'par', sc...  101 us
    another operation x14, other arithmetic, shards(): factor = jnp.linalg.cholesky(square_s)  78.7 us
    another operation x3, other arithmetic, shards(): jax.scipy.linalg.solve_triangular(factor, panel_s.T, lower=True)  39.5 us
    all_gather x1, waiting for transfers between devices, shards(): shared = lax.all_gather(reduced, 'par', axis=0, tiled=False)  34.7 us
    all_to_all x1, starting transfers between devices, shards(): shards_2 = lax.all_to_all(shards_2, 'smp', split_axis=0, concat_axis=0)  15.8 us
    reshape x1, local copies, waits for them, and re-layouts, shards(): main_parts.reshape(par_count * main_chunk, width)  13.1 us
  transfers between devices with their start and end apart: 4, of which 3 were waited for; matrix products, arithmetic and copies ran while one was open for 29% of the time, Pallas kernels for 0%

profile of v1, /device:TPU:1, one launch (start us, length us, event | category | flops | bytes accessed | tf_op | source)
XLA Modules:
  0.0 559.8 jit_solution(7416461256797841408)
XLA Ops:
  7.2 3.3 stack.2
  10.5 15.8 %all-to-all-start = ((bf16[16,256,512]{2,1,0:T(8,128)(2,1)}), bf16[16,256,512]{2,1,0:T(8,128)(2,1)}, u32[]{:S(2)}, u32[]{:S(2)}) async-start(bf16[16,256,512]{2,1,0:T(8,128)(2,1)} %stack.2), calls=%async_computation | async-start | bytes 8388608 | tf_op jit(solution)/shard_map/all_to_all | solution.py:23
  26.3 181.7 %all-to-all-done = bf16[16,256,512]{2,1,0:T(8,128)(2,1)} async-done(((bf16[16,256,512]{2,1,0:T(8,128)(2,1)}), bf16[16,256,512]{2,1,0:T(8,128)(2,1)}, u32[]{:S(2)}, u32[]{:S(2)}) %all-to-all-start) | async-done | bytes 4194336 | tf_op jit(solution)/shard_map/all_to_all | solution.py:23
  208.1 2.8 convert_reduce_fusion
  210.9 3.0 fusion
  213.9 2.0 copy-done
  216.5 3.5 fusion.23
  220.0 1.9 copy-done.1
  222.0 5.0 multiply_reduce_fusion
  226.9 0.6 broadcast_in_dim.46
  227.6 1.5 maximum_maximum_fusion
  229.2 100.6 %reduce-scatter.3.cloned.1.call-done = f32[56,256]{1,0:T(8,128)} async-done(((f32[1792,256]{1,0:T(8,128)}), f32[56,256]{1,0:T(8,128)}) %reduce-scatter.3.cloned.1.call-update) | async-done | bytes 57360 | tf_op jit(solution)/shard_map/reduce_scatter | solution.py:47
  329.9 1.4 broadcast_multiply_fusion.1
  331.4 8.0 %fusion.4 = f32[4096,512]{1,0:T(8,128)} fusion(bf16[4096,512]{1,0:T(8,128)(2,1)} %copy-done), kind=kOutput, calls=%fused_computation.32 | convolution fusion | flops 2147483648 | bytes 13107200 | tf_op jit(solution)/shard_map/dot_general | solution.py:33
  339.4 9.3 %reshape.110 = f32[32,256,256]{2,1,0:T(8,128)} reshape(f32[4096,512]{1,0:T(8,128)} %fusion.4) | data formatting | bytes 16777216 | tf_op jit(solution)/shard_map/reshape | solution.py:56
  348.7 10.5 %pad_maximum_fusion = f32[32,384,256]{2,1,0:T(8,128)} fusion(f32[32,256,256]{2,1,0:T(8,128)} %reshape.110, f32[32,128,256]{2,1,0:T(8,128)} %bitcast.79), kind=kLoop, calls=%fused_computation.2 | loop fusion | flops 3145728 | bytes 25165824 | tf_op jit(solution)/shard_map/concatenate | solution.py:53
  359.2 34.7 %all-gather.3.cloned.1.call-done = f32[1792,256]{1,0:T(8,128)} async-done(((f32[56,256]{1,0:T(8,128)}), f32[1792,256]{1,0:T(8,128)}) %all-gather.3.cloned.1.call-update) | async-done | bytes 1835024 | tf_op jit(solution)/shard_map/all_gather | solution.py:52
  393.9 13.1 %copy.43 = f32[12288,256]{0,1:T(8,128)} copy(f32[12288,256]{1,0:T(8,128)} %bitcast.78) | data formatting | bytes 25165824 | tf_op jit(solution)/shard_map/reshape | solution.py:64
  407.1 1.4 copy-done.3
  408.5 0.5 slice.171
  409.0 0.9 slice.172
  412.0 11.7 %cholesky.103 = f32[128,128]{1,0:T(8,128)S(1)} custom-call(f32[128,128]{1,0:T(8,128)S(1)} %cholesky.263), custom_call_target="Cholesky" | custom-call | tf_op jit(solution)/shard_map/jit(cholesky)/cholesky | solution.py:86
  423.8 9.8 %custom-call.34 = f32[1,128,128]{1,2,0:T(8,128)S(1)} custom-call(f32[1,128,128]{2,1,0:T(8,128)S(1)} %get-tuple-element.47), custom_call_target="InvertDiagBlocksLowerTriangular" | custom-call | tf_op jit(solution)/shard_map/jit(cholesky)/cholesky | solution.py:86
  434.5 11.7 %cholesky.215 = f32[128,128]{1,0:T(8,128)S(1)} custom-call(f32[128,128]{1,0:T(8,128)S(1)} %cholesky.267), custom_call_target="Cholesky" | custom-call | tf_op jit(solution)/shard_map/jit(cholesky)/cholesky | solution.py:86
  446.3 9.9 %custom-call.35 = f32[1,128,128]{1,2,0:T(8,128)S(1)} custom-call(f32[1,128,128]{2,1,0:T(8,128)S(1)} %get-tuple-element.45), custom_call_target="InvertDiagBlocksLowerTriangular" | custom-call | tf_op jit(solution)/shard_map/jit(cholesky)/cholesky | solution.py:86
  456.8 0.6 convolution_subtract_fusion.4
  457.4 11.7 %cholesky.236 = f32[128,128]{1,0:T(8,128)S(1)} custom-call(f32[128,128]{1,0:T(8,128)S(1)} %cholesky.272), custom_call_target="Cholesky" | custom-call | tf_op jit(solution)/shard_map/jit(cholesky)/cholesky | solution.py:86
  469.2 9.8 %custom-call.36 = f32[1,128,128]{1,2,0:T(8,128)S(1)} custom-call(f32[1,128,128]{2,1,0:T(8,128)S(1)} %get-tuple-element.43), custom_call_target="InvertDiagBlocksLowerTriangular" | custom-call | tf_op jit(solution)/shard_map/jit(cholesky)/cholesky | solution.py:86
  479.4 0.5 convolution_subtract_fusion.9
  479.8 11.9 %cholesky.253 = f32[128,128]{1,0:T(8,128)S(1)} custom-call(f32[128,128]{1,0:T(8,128)S(1)} %convolution_subtract_fusion.9), custom_call_target="Cholesky" | custom-call | tf_op jit(solution)/shard_map/jit(cholesky)/cholesky | solution.py:86
  491.9 0.6 compare_reduce_fusion.2
  493.7 0.6 compare_reduce_fusion.1
  495.0 0.6 compare_reduce_fusion
  496.5 8.1 %while.1 = (s32[]{:T(128)}, f32[512,512]{0,1:T(8,128)S(1)}, s32[4,2]{0,1:T(2,128)S(1)}, f32[4,128,128]{2,1,0:T(8,128)S(1)}, s32[]{:T(128)}) while((s32[]{:T(128)}, f32[512,512]{0,1:T(8,128)S(1)}, s32[4,2]{0,1:T(2,128)S(1)}, f32[4,128,128]{2,1,0:T(8,128)S(1)}, s32[]{:T(128)}) %tuple.35), condition=%wide.while_cond, body=%wide.while_body.sunk | while | flops 2 | bytes 393329 | solution.py:87
  496.6 0.5 fusion.79
  497.1 1.3 dynamic-slice.7
  498.6 0.5 fusion.79
  499.1 1.3 dynamic-slice.7
  500.6 0.5 fusion.79
  501.2 1.3 dynamic-slice.7
  502.7 0.5 fusion.79
  503.2 1.3 dynamic-slice.7
  504.6 39.3 %custom-call.37 = f32[4,128,128]{1,2,0:T(8,128)S(1)} custom-call(f32[4,128,128]{2,1,0:T(8,128)S(1)} %get-tuple-element.13), custom_call_target="InvertDiagBlocksLowerTriangular" | custom-call | tf_op jit(solution)/shard_map/jit(_solve_triangular)/triangular_solve | solution.py:87
  545.7 0.5 convolution_subtract_fusion.2
  546.6 1.0 copy.40
  547.6 1.0 broadcast_multiply_fusion
  550.6 0.5 convolution_subtract_fusion.8
  551.4 1.7 convolution_subtract_fusion.1
  (81 shorter events, 9.5 us)
Async XLA Ops:
  10.5 197.6 %all-to-all-start = ((bf16[16,256,512]{2,1,0:T(8,128)(2,1)}), bf16[16,256,512]{2,1,0:T(8,128)(2,1)}, u32[]{:S(2)}, u32[]{:S(2)}) async-start(bf16[16,256,512]{2,1,0:T(8,128)(2,1)} %stack.2), calls=%async_computation | async-start | bytes 8388608 | tf_op jit(solution)/shard_map/all_to_all | solution.py:23
  26.3 303.6 %reduce-scatter.3.cloned.1.call-start = ((), (), s32[]{:S(2)}) async-start(), calls=%async_computation.3 | async-start | bytes 1892352 | tf_op jit(solution)/shard_map/reduce_scatter | solution.py:47
  213.9 2.0 copy-start
  220.0 1.9 copy-start.1
  229.2 164.7 %all-gather.3.cloned.1.call-start = ((), (), s32[]{:S(2)}) async-start(), calls=%async_computation.5 | async-start | bytes 1892352 | tf_op jit(solution)/shard_map/all_gather | solution.py:52
  331.3 216.2 %reduce-scatter.5.cloned.1.call-start = ((), (), s32[]{:S(2)}) async-start(), calls=%async_computation.4 | async-start | bytes 12976128 | tf_op jit(solution)/shard_map/reduce_scatter | solution.py:63
  407.0 1.5 copy-start.3
  446.3 97.7 %copy-start.2 = (f32[32,16,256]{2,1,0:T(8,128)S(1)}, f32[32,16,256]{2,1,0:T(8,128)}, u32[]{:S(2)}) copy-start(f32[32,16,256]{2,1,0:T(8,128)} %slice.172) | copy-start | bytes 1572868
Sparse Core Ops, SparseCore 0:
  229.3 100.4 reduce-scatter.2
  333.6 60.3 all-gather.2
  407.1 125.6 reduce-scatter.4
